TPU v7x, 32 devices: a whole 2x2x4 slice. The times are simulated.
32 devices in a mesh: lon: 8 (over y, x, core), lat: 4 (over z).
Axes of the slice: x: 2, y: 2, z: 4, core: 2. Of those that a mesh axis runs over, the one named last changes fastest.
Arguments:
- obs_rows: bfloat16 [131072, 128], P(('lon', 'lat')), may hold values from -6 to 6
- cell_ids: int32 [131072], P(('lon', 'lat')), may hold values from 0 to 511
- counts: int32 [32, 32], P(('lon', 'lat')), may hold values from 16 to 128, as said below
- w_embed: bfloat16 [128, 256], replicated, may hold values from -0.5 to 0.5
- w_density: bfloat16 [256], replicated, may hold values from -3 to 3
- kernels: bfloat16 [3, 3, 3, 256, 256], replicated, may hold values from -0.125 to 0.125
- cotangent: bfloat16 [64, 256, 256], P('lat', 'lon'), may hold values from -6 to 6
Outputs:
- encoded: bfloat16 [64, 256, 256], P('lat', 'lon')
- grad_kernels: bfloat16 [3, 3, 3, 256, 256], replicated
- grad_embed: bfloat16 [128, 256], replicated
- grad_obs: bfloat16 [131072, 128], P(('lon', 'lat'))
Inputs may be any that keep to these rules, and one draw needn't show every extreme that they name: `counts`: the live rows of each slot are its first ones; in every draw some tile owner receives 128 live rows from every device.
All inputs are finite; a program needn't handle non-finite values.
Results may differ from a plain program's by a relative error of at most 0.011.
Values may be sent and summed in bfloat16 or wider, within the bound.
No kernel may reach another device: no remote copies, remote signals or barrier semaphores. Data moves between devices by JAX's collectives and lax.ppermute only.
A program may use at most 128 MiB of HBM per device.

v0:
```python
import math
import jax
import jax.numpy as jnp
from jax import lax
from jax.sharding import PartitionSpec as P

ID_BASE = 128


def shift_pairs(count, step, periodic):
    pairs = []
    for source in range(count):
        target = source + step
        if 0 <= target < count:
            pairs.append((source, target))
        elif periodic:
            pairs.append((source, target % count))
    return pairs


def widen(block, depth):
    lon_count = lax.axis_size("lon")
    lat_count = lax.axis_size("lat")
    west = lax.ppermute(block[:, -depth:], "lon", shift_pairs(lon_count, 1, True))
    east = lax.ppermute(block[:, :depth], "lon", shift_pairs(lon_count, -1, True))
    block = jnp.concatenate([west, block, east], axis=1)
    north = lax.ppermute(block[-depth:], "lat", shift_pairs(lat_count, 1, False))
    south = lax.ppermute(block[:depth], "lat", shift_pairs(lat_count, -1, False))
    return jnp.concatenate([north, block, south], axis=0)


def lat_mask(rows, margin, height):
    lat_index = lax.axis_index("lat")
    lat_count = lax.axis_size("lat")
    global_row = lat_index * height - margin + jnp.arange(rows, dtype=jnp.int32)
    return ((global_row >= 0) & (global_row < lat_count * height))[:, None, None]


def crop(field, margin):
    if margin == 0:
        return field
    return field[margin:-margin, margin:-margin]


def conv_valid(padded, kernel):
    return lax.conv_general_dilated(
        padded[None],
        kernel,
        (1, 1),
        "VALID",
        dimension_numbers=("NHWC", "HWIO", "NHWC"),
        preferred_element_type=jnp.float32,
    )[0]


def reduce_replicated(parts):
    flat = jnp.concatenate([part.reshape(-1) for part in parts])
    summed = lax.psum_scatter(flat, ("lon", "lat"), scatter_dimension=0, tiled=True)
    return summed


def on_device(obs_rows, cell_ids, counts, w_embed, w_density, kernels, cotangent):
    lon_count = lax.axis_size("lon")
    lat_count = lax.axis_size("lat")
    devices = lon_count * lat_count
    height, tile_width, channels = cotangent.shape
    cell_count = height * tile_width
    slot_rows = obs_rows.shape[0] // devices
    feat_count = obs_rows.shape[1]
    layer_count = kernels.shape[0]
    margin = 2 * layer_count
    cot_wide = widen(cotangent, layer_count)
    live_mask = jnp.arange(slot_rows, dtype=jnp.int32)[None, :] < counts[0][:, None]
    slot_ids = cell_ids.reshape(devices, slot_rows)
    id_high = jnp.where(live_mask, slot_ids // ID_BASE, -1)
    id_low = jnp.where(live_mask, slot_ids % ID_BASE, -1)
    code = jnp.concatenate([id_high, id_low], axis=1).astype(jnp.bfloat16)
    code_rows = -(-2 * slot_rows // feat_count)
    code_pad = -(-code_rows // 16) * 16
    code = jnp.pad(code, ((0, 0), (0, code_rows * feat_count - 2 * slot_rows)))
    code = code.reshape(devices, code_rows, feat_count)
    code = jnp.pad(code, ((0, 0), (0, code_pad - code_rows), (0, 0)))
    packed = jnp.concatenate([obs_rows.reshape(devices, slot_rows, feat_count), code], axis=1)
    got = lax.all_to_all(packed, ("lon", "lat"), split_axis=0, concat_axis=0, tiled=True)
    got_rows = got[:, :slot_rows].reshape(devices * slot_rows, feat_count)
    got_code = got[:, slot_rows : slot_rows + code_rows].reshape(devices, code_rows * feat_count)
    got_code = got_code.astype(jnp.int32)
    got_ids = (got_code[:, :slot_rows] * ID_BASE + got_code[:, slot_rows : 2 * slot_rows]).reshape(
        -1
    )
    cell_iota = jnp.arange(cell_count, dtype=jnp.int32)
    onehot = (got_ids[:, None] == cell_iota[None, :]).astype(jnp.bfloat16)
    cell_sums = lax.dot_general(
        onehot, got_rows, (((0,), (0,)), ((), ())), preferred_element_type=jnp.float32
    )
    density = jnp.sum(onehot.astype(jnp.float32), axis=0)
    inv_root = lax.rsqrt(density + 1.0)
    features = (cell_sums * inv_root[:, None]).astype(jnp.bfloat16)
    start_act = (
        jnp.dot(features, w_embed, preferred_element_type=jnp.float32)
        + jnp.log1p(density)[:, None] * w_density.astype(jnp.float32)[None, :]
    )
    activation = start_act.astype(jnp.bfloat16).reshape(height, tile_width, channels)
    act = widen(activation, margin)
    stored_acts = [act]
    stored_pre = []
    for layer_index in range(layer_count):
        out_margin = margin - layer_index - 1
        preact = conv_valid(act, kernels[layer_index])
        act = (crop(act, 1).astype(jnp.float32) + jax.nn.silu(preact)).astype(jnp.bfloat16)
        act = jnp.where(lat_mask(act.shape[0], out_margin, height), act, jnp.zeros_like(act))
        stored_pre.append(preact)
        stored_acts.append(act)
    encoded = crop(act, margin - layer_count)
    grad_scale = 1.0 / math.sqrt(cell_count * devices)
    back = cot_wide
    reduced = [None] * layer_count
    for layer_index in reversed(range(layer_count)):
        back_margin = layer_index + 1
        preact = crop(stored_pre[layer_index], margin - layer_index - 1 - back_margin)
        sigmoid_v = jax.nn.sigmoid(preact)
        slope = (
            back.astype(jnp.float32) * (sigmoid_v * (1.0 + preact * (1.0 - sigmoid_v)))
        ).astype(jnp.bfloat16)
        slope = jnp.where(
            lat_mask(slope.shape[0], back_margin, height), slope, jnp.zeros_like(slope)
        )
        slope_flat = crop(slope, back_margin).reshape(cell_count, channels)
        act_in = crop(stored_acts[layer_index], margin - layer_index - 1)
        tap_rows = []
        for row_off in range(3):
            tap_cols = []
            for col_off in range(3):
                window = act_in[row_off : row_off + height, col_off : col_off + tile_width].reshape(
                    cell_count, channels
                )
                tap_cols.append(
                    lax.dot_general(
                        window,
                        slope_flat,
                        (((0,), (0,)), ((), ())),
                        preferred_element_type=jnp.float32,
                    )
                )
            tap_rows.append(jnp.stack(tap_cols))
        tap_grad = jnp.stack(tap_rows)
        flipped = jnp.transpose(kernels[layer_index][::-1, ::-1], (0, 1, 3, 2))
        spread = conv_valid(slope, flipped)
        back = lax.optimization_barrier(
            (crop(back, 1).astype(jnp.float32) + spread).astype(jnp.bfloat16)
        )
        if layer_index > 0:
            reduced[layer_index] = reduce_replicated([tap_grad])
        else:
            last_grad = tap_grad
    back_flat = back.reshape(cell_count, channels)
    embed_grad = lax.dot_general(
        features, back_flat, (((0,), (0,)), ((), ())), preferred_element_type=jnp.float32
    )
    reduced[0] = reduce_replicated([last_grad, embed_grad])
    cell_grad = (
        lax.dot_general(
            back_flat, w_embed, (((1,), (1,)), ((), ())), preferred_element_type=jnp.float32
        )
        * inv_root[:, None]
    ).astype(jnp.bfloat16)
    picked = jnp.dot(onehot, cell_grad, preferred_element_type=jnp.float32).astype(jnp.bfloat16)
    grad_obs = lax.all_to_all(picked, ("lon", "lat"), split_axis=0, concat_axis=0, tiled=True)
    tap_size = kernels[0].size
    gathered = [
        lax.all_gather((part * grad_scale).astype(jnp.bfloat16), ("lon", "lat"), axis=0, tiled=True)
        for part in reduced
    ]
    kernel_out = jnp.stack(
        [gathered[0][:tap_size]] + [gathered[index] for index in range(1, layer_count)]
    ).reshape(kernels.shape)
    embed_out = gathered[0][tap_size:].reshape(w_embed.shape)
    return (encoded, kernel_out, embed_out, grad_obs)


def solution(mesh):
    placed = (
        P(("lon", "lat"), None),
        P(("lon", "lat")),
        P(("lon", "lat"), None),
        P(),
        P(),
        P(),
        P("lat", "lon", None),
    )
    return jax.shard_map(
        on_device,
        mesh=mesh,
        in_specs=placed,
        out_specs=(P("lat", "lon", None), P(), P(), P(("lon", "lat"), None)),
        check_vma=False,
    )
```

profile of v0, /device:TPU:0, one launch (start us, length us, event | category | flops | bytes accessed | tf_op | source)
XLA Modules:
  0.0 475.4 jit_solution(3114485129641464012)
XLA Ops:
  7.2 0.9 fusion.119
  8.9 2.3 pad_maximum_fusion.5
  11.2 7.3 %all-to-all-start = ((bf16[32,144,128]{2,1,0:T(8,128)(2,1)}), bf16[32,144,128]{2,1,0:T(8,128)(2,1)S(1)}, u32[]{:S(2)}, u32[]{:S(2)}) async-start(bf16[32,144,128]{2,1,0:T(8,128)(2,1)} %pad_maximum_fusion.5), calls=%async_computation | async-start | bytes 2359296 | tf_op jit(solution)/shard_map/all_to_all | solution.py:84
  18.6 2.5 collective-permute-start.5
  21.7 4.4 collective-permute-done.5
  26.1 2.8 collective-permute-done.4
  28.9 0.9 fusion.160
  29.8 16.5 %all-to-all-done = bf16[32,144,128]{2,1,0:T(8,128)(2,1)S(1)} async-done(((bf16[32,144,128]{2,1,0:T(8,128)(2,1)}), bf16[32,144,128]{2,1,0:T(8,128)(2,1)S(1)}, u32[]{:S(2)}, u32[]{:S(2)}) %all-to-all-start) | async-done | bytes 1179680 | tf_op jit(solution)/shard_map/all_to_all | solution.py:84
  46.3 1.0 convert_reduce_fusion
  47.5 3.0 fusion.19
  50.7 2.7 collective-permute-start.1
  53.4 1.3 collective-permute-start.7
  54.7 4.6 collective-permute-start.6
  59.5 1.3 collective-permute-start.3
  60.8 4.6 collective-permute-start.2
  65.9 0.9 pad_maximum_fusion.8
  67.2 1.2 collective-permute-done.2
  69.7 2.9 convolution_select_fusion
  73.3 1.1 pad_maximum_fusion.6
  75.0 0.9 pad.7
  75.9 1.8 reshape.308
  77.9 2.8 convolution_select_fusion.1
  82.5 1.0 copy-done.18
  83.5 1.3 add_multiply_fusion
  86.6 1.2 fusion.84
  91.0 0.9 copy-done.5
  93.0 1.2 convolution_select_fusion.3
  99.1 1.1 convolution_select_fusion.4
  104.2 2.6 copy.118
  107.1 2.7 copy.117
  110.5 1.0 convolution_select_fusion.5
  114.1 1.2 copy.115
  115.4 1.6 pad_maximum_fusion.1
  117.0 166.5 %all-reduce.7.cloned.1.call-done = (f32[589824]{0:T(1024)}, f32[589824]{0:T(1024)}, f32[622592]{0:T(1024)}) async-done(((f32[589824]{0:T(1024)}, f32[589824]{0:T(1024)}, f32[622592]{0:T(1024)}), (f32[589824]{0:T(1024)}, f32[589824]{0:T(1024)}, f32[622592]{0:T(1024)})) %all-reduce.7.cloned.1.call-update) | async-done | bytes 7208976
  283.5 1.5 fusion.117
  285.1 1.5 fusion.118
  286.7 1.5 fusion.116
  288.2 1.7 fusion.3
  290.0 30.8 %all_to_all.17 = bf16[32,128,128]{2,1,0:T(8,128)(2,1)S(1)} all-to-all(bf16[32,128,128]{2,1,0:T(8,128)(2,1)S(1)} %bitcast.273), channel_id=1, replica_groups=mesh['lon'=8,'lat'=4] {'lon','lat'}, dimensions={0} | all-to-all | bytes 2097152 | tf_op jit(solution)/shard_map/all_to_all | solution.py:168
  320.8 24.1 %all-gather.8.cloned.1.call-done = bf16[589824]{0:T(1024)(128)(2,1)} async-done(((bf16[18432]{0:T(1024)(128)(2,1)}), bf16[589824]{0:T(1024)(128)(2,1)}) %all-gather.8.cloned.1.call-update) | async-done | bytes 1179664 | tf_op jit(solution)/shard_map/all_gather | solution.py:171
  344.9 2.2 stack.206
  347.1 54.6 %all-gather.6.cloned.1.call-done = bf16[589824]{0:T(1024)(128)(2,1)} async-done(((bf16[18432]{0:T(1024)(128)(2,1)}), bf16[589824]{0:T(1024)(128)(2,1)}) %all-gather.6.cloned.1.call-update) | async-done | bytes 1179664 | tf_op jit(solution)/shard_map/all_gather | solution.py:171
  401.7 2.2 stack.189
  403.9 54.7 %all-gather.4.cloned.1.call-done = bf16[622592]{0:T(1024)(128)(2,1)} async-done(((bf16[19456]{0:T(1024)(128)(2,1)}), bf16[622592]{0:T(1024)(128)(2,1)}) %all-gather.4.cloned.1.call-update) | async-done | bytes 1245200 | tf_op jit(solution)/shard_map/all_gather | solution.py:171
  458.6 2.4 slice.329
  461.0 3.0 stack.172
  464.7 3.0 pad_maximum_fusion
  467.7 1.0 copy.155
  (175 shorter events, 26.3 us)
Async XLA Ops:
  7.2 43.3 %copy-start = (bf16[128,256]{1,0:T(8,128)(2,1)S(1)}, bf16[128,256]{1,0:T(8,128)(2,1)}, u32[]{:S(2)}) copy-start(bf16[128,256]{1,0:T(8,128)(2,1)} %param.10) | copy-start | bytes 196612
  11.2 7.4 %copy-start.4 = (bf16[16,32,256]{2,1,0:T(8,128)(2,1)S(1)}, bf16[16,32,256]{2,1,0:T(8,128)(2,1)}, u32[]{:S(2)}) copy-start(bf16[16,32,256]{2,1,0:T(8,128)(2,1)} %param.13) | copy-start | bytes 786436
  11.2 10.4 %copy-start.19 = (bf16[256]{0:T(256)(128)(2,1)S(1)}, bf16[256]{0:T(256)(128)(2,1)}, u32[]{:S(2)}) copy-start(bf16[256]{0:T(256)(128)(2,1)} %param.11) | copy-start | bytes 1540
  11.2 35.1 %all-to-all-start = ((bf16[32,144,128]{2,1,0:T(8,128)(2,1)}), bf16[32,144,128]{2,1,0:T(8,128)(2,1)S(1)}, u32[]{:S(2)}, u32[]{:S(2)}) async-start(bf16[32,144,128]{2,1,0:T(8,128)(2,1)} %pad_maximum_fusion.5), calls=%async_computation | async-start | bytes 2359296 | tf_op jit(solution)/shard_map/all_to_all | solution.py:84
  18.5 265.0 %all-reduce.7.cloned.1.call-start = ((), (), s32[]{:S(2)}) async-start(), calls=%async_computation.5 | async-start | bytes 14417920
  18.6 7.5 %collective-permute-start.5 = (bf16[16,3,256]{2,1,0:T(4,128)(2,1)S(1)}, bf16[16,3,256]{2,1,0:T(4,128)(2,1)S(1)}, u32[]{:S(2)}, u32[]{:S(2)}) collective-permute-start(bf16[16,3,256]{2,1,0:T(4,128)(2,1)S(1)} %get-tuple-element.22), channel_id=1, source_target_pairs={{0,28},{4,0},{8,4},{12,8},{16,12},{20,16},{24,20},{28,24},{1,29},{... | collective-permute-start | bytes 73736 | tf_op jit(solution)/shard_map/ppermute | solution.py:25
  21.1 7.8 %collective-permute-start.4 = (bf16[16,3,256]{2,1,0:T(4,128)(2,1)S(1)}, bf16[16,3,256]{2,1,0:T(4,128)(2,1)S(1)}, u32[]{:S(2)}, u32[]{:S(2)}) collective-permute-start(bf16[16,3,256]{2,1,0:T(4,128)(2,1)S(1)} %get-tuple-element.21), channel_id=1, source_target_pairs={{0,4},{4,8},{8,12},{12,16},{16,20},{20,24},{24,28},{28,0},{1,5},{5... | collective-permute-start | bytes 73736 | tf_op jit(solution)/shard_map/ppermute | solution.py:24
  21.6 43.7 %copy-start.14 = (pred[22]{0:T(512)(128)(4,1)}, pred[22]{0:T(512)(128)(4,1)S(1)}, u32[]{:S(2)}) copy-start(pred[22]{0:T(512)(128)(4,1)S(1)} %compare_and_fusion.4) | copy-start | bytes 70
  50.4 9.0 %copy-start.8 = (bf16[512,128]{1,0:T(8,128)(2,1)}, bf16[512,128]{1,0:T(8,128)(2,1)S(1)}, u32[]{:S(2)}) copy-start(bf16[512,128]{1,0:T(8,128)(2,1)S(1)} %fusion.19) | copy-start | bytes 393220
  50.7 8.6 %collective-permute-start.1 = (bf16[16,6,256]{2,1,0:T(8,128)(2,1)S(1)}, bf16[16,6,256]{2,1,0:T(8,128)(2,1)S(1)}, u32[]{:S(2)}, u32[]{:S(2)}) collective-permute-start(bf16[16,6,256]{2,1,0:T(8,128)(2,1)S(1)} %get-tuple-element.24), channel_id=1, source_target_pairs={{0,28},{4,0},{8,4},{12,8},{16,12},{20,16},{24,20},{28,24},{1,29},{... | collective-permute-start | bytes 147464 | tf_op jit(solution)/shard_map/ppermute | solution.py:25
  53.4 5.9 %collective-permute-start = (bf16[16,6,256]{2,1,0:T(8,128)(2,1)S(1)}, bf16[16,6,256]{2,1,0:T(8,128)(2,1)S(1)}, u32[]{:S(2)}, u32[]{:S(2)}) collective-permute-start(bf16[16,6,256]{2,1,0:T(8,128)(2,1)S(1)} %get-tuple-element.23), channel_id=1, source_target_pairs={{0,4},{4,8},{8,12},{12,16},{16,20},{20,24},{24,28},{28,0},{1,5},{5... | collective-permute-start | bytes 147464 | tf_op jit(solution)/shard_map/ppermute | solution.py:24
  53.4 12.5 %collective-permute-start.7 = (bf16[3,38,256]{2,1,0:T(8,128)(2,1)S(1)}, bf16[3,38,256]{2,1,0:T(8,128)(2,1)S(1)}, u32[]{:S(2)}, u32[]{:S(2)}) collective-permute-start(bf16[3,38,256]{2,1,0:T(8,128)(2,1)S(1)} %get-tuple-element.20), channel_id=1, source_target_pairs={{1,0},{2,1},{3,2},{5,4},{6,5},{7,6},{9,8},{10,9},{11,10},{13,12},{... | collective-permute-start | bytes 175112 | tf_op jit(solution)/shard_map/ppermute | solution.py:28
  54.7 11.2 %collective-permute-start.6 = (bf16[3,38,256]{2,1,0:T(8,128)(2,1)S(1)}, bf16[3,38,256]{2,1,0:T(8,128)(2,1)S(1)}, u32[]{:S(2)}, u32[]{:S(2)}) collective-permute-start(bf16[3,38,256]{2,1,0:T(8,128)(2,1)S(1)} %get-tuple-element.19), channel_id=1, source_target_pairs={{0,1},{1,2},{2,3},{4,5},{5,6},{6,7},{8,9},{9,10},{10,11},{12,13},{... | collective-permute-start | bytes 175112 | tf_op jit(solution)/shard_map/ppermute | solution.py:27
  59.3 9.2 %copy-start.6 = (bf16[16,6,256]{2,1,0:T(8,128)(2,1)}, bf16[16,6,256]{2,1,0:T(8,128)(2,1)S(1)}, u32[]{:S(2)}) copy-start(bf16[16,6,256]{2,1,0:T(8,128)(2,1)S(1)} %collective-permute-done) | copy-start | bytes 147460
  59.5 7.7 %collective-permute-start.3 = (bf16[6,44,256]{2,1,0:T(8,128)(2,1)S(1)}, bf16[6,44,256]{2,1,0:T(8,128)(2,1)S(1)}, u32[]{:S(2)}, u32[]{:S(2)}) collective-permute-start(bf16[6,44,256]{2,1,0:T(8,128)(2,1)S(1)} %get-tuple-element.16), channel_id=1, source_target_pairs={{1,0},{2,1},{3,2},{5,4},{6,5},{7,6},{9,8},{10,9},{11,10},{13,12},{... | collective-permute-start | bytes 405512 | tf_op jit(solution)/shard_map/ppermute | solution.py:28
  60.8 7.6 %collective-permute-start.2 = (bf16[6,44,256]{2,1,0:T(8,128)(2,1)S(1)}, bf16[6,44,256]{2,1,0:T(8,128)(2,1)S(1)}, u32[]{:S(2)}, u32[]{:S(2)}) collective-permute-start(bf16[6,44,256]{2,1,0:T(8,128)(2,1)S(1)} %get-tuple-element.15), channel_id=1, source_target_pairs={{0,1},{1,2},{2,3},{4,5},{5,6},{6,7},{8,9},{9,10},{10,11},{12,13},{... | collective-permute-start | bytes 405512 | tf_op jit(solution)/shard_map/ppermute | solution.py:27
  65.9 2.9 copy-start.10
  65.9 2.9 copy-start.12
  68.4 0.7 copy-start.2
  69.0 0.7 copy-start.25
  73.3 1.1 copy-start.16
  75.9 2.0 copy-start.24
  81.5 2.0 copy-start.18
  82.1 1.3 copy-start.23
  85.6 1.0 copy-start.1
  85.6 1.0 copy-start.17
  90.9 1.0 copy-start.5
  90.9 1.0 copy-start.11
  91.0 1.0 copy-start.13
  91.0 1.0 copy-start.15
  92.3 0.7 copy-start.22
  98.4 0.7 copy-start.21
  100.5 0.9 copy-start.3
  100.5 0.9 copy-start.7
  109.8 0.7 copy-start.20
  111.7 0.9 copy-start.9
  117.0 227.9 %all-gather.8.cloned.1.call-start = ((), (), s32[]{:S(2)}) async-start(), calls=%async_computation.4 | async-start | bytes 1216512 | tf_op jit(solution)/shard_map/all_gather | solution.py:171
  285.1 116.6 %all-gather.6.cloned.1.call-start = ((), (), s32[]{:S(2)}) async-start(), calls=%async_computation.3 | async-start | bytes 1216512 | tf_op jit(solution)/shard_map/all_gather | solution.py:171
  286.7 172.0 %all-gather.4.cloned.1.call-start = ((), (), s32[]{:S(2)}) async-start(), calls=%async_computation.2 | async-start | bytes 1284096 | tf_op jit(solution)/shard_map/all_gather | solution.py:171
  461.0 3.0 slice-start
Sparse Core Ops, SparseCore 0:
  117.1 166.3 all-reduce.6
  287.3 57.5 all-gather.7
  348.6 53.0 all-gather.5
  405.5 53.1 all-gather.3
where the time goes:
time: 484 us; the launch traced here: 475 us
  waiting for transfers between devices  325 us (67%)
  local copies, waits for them, and re-layouts  31.8 us (7%)
  blocking collectives  30.8 us (6%)
  other arithmetic  24.4 us (5%)
  starting transfers between devices  24.4 us (5%)
  matrix products  23.7 us (5%)
  between operations  15.1 us (3%)
    unnamed x5, waiting for transfers between devices  167 us
    all_gather x3, waiting for transfers between devices, on_device(): lax.all_gather((part * grad_scale).astype(jnp.bfloat16), ('lon', 'lat'),...  133 us
    all_to_all x1, blocking collectives, on_device(): lax.all_to_all(picked, ('lon', 'lat'), split_axis=0, concat_axis=0, tiled...  30.8 us
    all_to_all x1, waiting for transfers between devices, on_device(): lax.all_to_all(packed, ('lon', 'lat'), split_axis=0, concat_axis=0, tiled...  16.5 us
    unnamed x63, local copies, waits for them, and re-layouts  13.4 us
    conv_general_dilated x6, matrix products, conv_valid(): lax.conv_general_dilated(padded[None], kernel, (1, 1), 'VALID', dimension...  10.2 us
  transfers between devices with their start and end apart: 13, of which 9 were waited for; matrix products, arithmetic and copies ran while one was open for 3% of the time, Pallas kernels for 0%

commit v1 on v0

--- a/solution.py
+++ b/solution.py
@@ -5,6 +5,30 @@
 from jax.sharding import PartitionSpec as P
 
 ID_BASE = 128
+
+
+def point_task_on_mesh(block_in):
+    m_next, fresh, v1 = (
+        lax.axis_size(("lon", "lat")),
+        lax.axis_index(("lon", "lat")),
+        block_in.shape[0],
+    )
+    current_block, k_now = (block_in, 1)
+    while k_now < m_next:
+        current_block = jnp.concatenate(
+            [
+                current_block,
+                lax.ppermute(
+                    current_block,
+                    ("lon", "lat"),
+                    [(j0, (j0 - k_now) % m_next) for j0 in range(m_next)],
+                ),
+            ],
+            axis=0,
+        )
+        k_now = 2 * k_now
+    x_new = jnp.roll(current_block, fresh * v1, axis=0)
+    return x_new
 
 
 def shift_pairs(count, step, periodic):
@@ -167,10 +191,7 @@
     picked = jnp.dot(onehot, cell_grad, preferred_element_type=jnp.float32).astype(jnp.bfloat16)
     grad_obs = lax.all_to_all(picked, ("lon", "lat"), split_axis=0, concat_axis=0, tiled=True)
     tap_size = kernels[0].size
-    gathered = [
-        lax.all_gather((part * grad_scale).astype(jnp.bfloat16), ("lon", "lat"), axis=0, tiled=True)
-        for part in reduced
-    ]
+    gathered = [point_task_on_mesh((part * grad_scale).astype(jnp.bfloat16)) for part in reduced]
     kernel_out = jnp.stack(
         [gathered[0][:tap_size]] + [gathered[index] for index in range(1, layer_count)]
     ).reshape(kernels.shape)

time: 484 us -> 423 us (0.87)
  the two profiles are of different devices: /device:TPU:0 before, /device:TPU:27 now
where the time goes in v1:
time: 423 us; the launch traced here: 415 us
  waiting for transfers between devices  263 us (62%)
  local copies, waits for them, and re-layouts  42.3 us (10%)
  starting transfers between devices  36.1 us (9%)
  other arithmetic  33.1 us (8%)
  matrix products  24.9 us (6%)
  between operations  15.6 us (4%)
    unnamed x2, waiting for transfers between devices  145 us
    ppermute x15, waiting for transfers between devices, point_task_on_mesh(): lax.ppermute(current_block, ('lon', 'lat'), [(j0, (j0 - k_now) % m_next)...  57.7 us
    all_to_all x1, waiting for transfers between devices, on_device(): lax.all_to_all(picked, ('lon', 'lat'), split_axis=0, concat_axis=0, tiled...  34.2 us
    unnamed x93, local copies, waits for them, and re-layouts  21.4 us
    all_to_all x1, waiting for transfers between devices, on_device(): lax.all_to_all(packed, ('lon', 'lat'), split_axis=0, concat_axis=0, tiled...  14.3 us
    conv_general_dilated x6, matrix products, conv_valid(): lax.conv_general_dilated(padded[None], kernel, (1, 1), 'VALID', dimension...  10.2 us
    concatenate x2, other arithmetic, point_task_on_mesh(): x_new = jnp.roll(current_block, fresh * v1, axis=0)  10 us
    ppermute x15, starting transfers between devices, point_task_on_mesh(): lax.ppermute(current_block, ('lon', 'lat'), [(j0, (j0 - k_now) % m_next)...  9.13 us
  transfers between devices with their start and end apart: 26, of which 20 were waited for; matrix products, arithmetic and copies ran while one was open for 6% of the time, Pallas kernels for 0%

profile of v1, /device:TPU:27, one launch (start us, length us, event | category | flops | bytes accessed | tf_op | source)
XLA Modules:
  0.0 415.0 jit_solution(7402610779682844918)
XLA Ops:
  8.9 2.3 pad_maximum_fusion.5
  11.2 6.2 %all-to-all-start = ((bf16[32,144,128]{2,1,0:T(8,128)(2,1)}), bf16[32,144,128]{2,1,0:T(8,128)(2,1)S(1)}, u32[]{:S(2)}, u32[]{:S(2)}) async-start(bf16[32,144,128]{2,1,0:T(8,128)(2,1)} %pad_maximum_fusion.5), calls=%async_computation | async-start | bytes 2359296 | tf_op jit(solution)/shard_map/all_to_all | solution.py:108
  17.9 2.3 collective-permute-start.4
  20.7 7.6 %collective-permute-done.5 = bf16[16,3,256]{2,1,0:T(4,128)(2,1)S(1)} collective-permute-done((bf16[16,3,256]{2,1,0:T(4,128)(2,1)S(1)}, bf16[16,3,256]{2,1,0:T(4,128)(2,1)S(1)}, u32[]{:S(2)}, u32[]{:S(2)}) %collective-permute-start.5) | collective-permute-done | bytes 24608 | tf_op jit(solution)/shard_map/ppermute | solution.py:49
  29.3 14.3 %all-to-all-done = bf16[32,144,128]{2,1,0:T(8,128)(2,1)S(1)} async-done(((bf16[32,144,128]{2,1,0:T(8,128)(2,1)}), bf16[32,144,128]{2,1,0:T(8,128)(2,1)S(1)}, u32[]{:S(2)}, u32[]{:S(2)}) %all-to-all-start) | async-done | bytes 1179680 | tf_op jit(solution)/shard_map/all_to_all | solution.py:108
  44.8 3.0 fusion.21
  48.0 1.6 collective-permute-start.1
  50.7 3.4 collective-permute-start.7
  54.1 1.3 collective-permute-start.6
  55.6 4.0 collective-permute-start.3
  59.6 1.3 collective-permute-start.2
  62.4 4.0 collective-permute-done.2
  67.8 2.9 convolution_select_fusion
  74.0 1.5 reshape.308
  75.7 2.8 convolution_select_fusion.1
  81.3 1.3 add_multiply_fusion
  84.4 1.2 fusion.86
  102.2 2.6 copy.118
  105.2 2.6 copy.117
  113.3 1.6 pad_maximum_fusion.1
  115.0 2.7 fusion.3
  117.7 5.4 %all-to-all-start.1 = ((bf16[32,128,128]{2,1,0:T(8,128)(2,1)}), bf16[32,128,128]{2,1,0:T(8,128)(2,1)S(1)}, u32[]{:S(2)}, u32[]{:S(2)}) async-start(bf16[32,128,128]{2,1,0:T(8,128)(2,1)} %bitcast.105), calls=%async_computation.1 | async-start | bytes 2097152 | tf_op jit(solution)/shard_map/all_to_all | solution.py:192
  123.1 34.2 %all-to-all-done.1 = bf16[32,128,128]{2,1,0:T(8,128)(2,1)S(1)} async-done(((bf16[32,128,128]{2,1,0:T(8,128)(2,1)}), bf16[32,128,128]{2,1,0:T(8,128)(2,1)S(1)}, u32[]{:S(2)}, u32[]{:S(2)}) %all-to-all-start.1) | async-done | bytes 1048608 | tf_op jit(solution)/shard_map/all_to_all | solution.py:192
  157.3 145.0 %all-reduce.7.cloned.1.call-done = (f32[589824]{0:T(1024)}, f32[589824]{0:T(1024)}, f32[622592]{0:T(1024)}) async-done(((f32[589824]{0:T(1024)}, f32[589824]{0:T(1024)}, f32[622592]{0:T(1024)}), (f32[589824]{0:T(1024)}, f32[589824]{0:T(1024)}, f32[622592]{0:T(1024)})) %all-reduce.7.cloned.1.call-update) | async-done | bytes 7208976
  305.4 1.5 constant_dynamic-update-slice_fusion
  307.8 2.4 collective-permute-done.18
  310.2 1.5 collective-permute-start.19
  312.1 1.9 collective-permute-done.8
  314.9 7.3 %collective-permute-done.19 = bf16[36864]{0:T(1024)(128)(2,1)S(1)} collective-permute-done((bf16[36864]{0:T(1024)(128)(2,1)S(1)}, bf16[36864]{0:T(1024)(128)(2,1)S(1)}, u32[]{:S(2)}, u32[]{:S(2)}) %collective-permute-start.19) | collective-permute-done | bytes 73760 | tf_op jit(solution)/shard_map/ppermute | solution.py:21
  322.2 1.5 collective-permute-done.14
  325.4 2.2 collective-permute-done.20
  327.7 1.5 collective-permute-done.15
  332.6 5.1 %collective-permute-done.21 = bf16[147456]{0:T(1024)(128)(2,1)S(1)} collective-permute-done((bf16[147456]{0:T(1024)(128)(2,1)S(1)}, bf16[147456]{0:T(1024)(128)(2,1)S(1)}, u32[]{:S(2)}, u32[]{:S(2)}) %collective-permute-start.21) | collective-permute-done | bytes 294944 | tf_op jit(solution)/shard_map/ppermute | solution.py:21
  337.8 1.3 collective-permute-start.22
  339.0 5.0 %collective-permute-done.16 = bf16[147456]{0:T(1024)(128)(2,1)S(1)} collective-permute-done((bf16[147456]{0:T(1024)(128)(2,1)S(1)}, bf16[147456]{0:T(1024)(128)(2,1)S(1)}, u32[]{:S(2)}, u32[]{:S(2)}) %collective-permute-start.16) | collective-permute-done | bytes 294944 | tf_op jit(solution)/shard_map/ppermute | solution.py:21
  344.1 1.3 collective-permute-start.17
  345.4 4.9 %collective-permute-done.11 = bf16[155648]{0:T(1024)(128)(2,1)S(1)} collective-permute-done((bf16[155648]{0:T(1024)(128)(2,1)S(1)}, bf16[155648]{0:T(1024)(128)(2,1)S(1)}, u32[]{:S(2)}, u32[]{:S(2)}) %collective-permute-start.11) | collective-permute-done | bytes 311328 | tf_op jit(solution)/shard_map/ppermute | solution.py:21
  352.5 10.6 %collective-permute-done.22 = bf16[294912]{0:T(1024)(128)(2,1)S(1)} collective-permute-done((bf16[294912]{0:T(1024)(128)(2,1)S(1)}, bf16[294912]{0:T(1024)(128)(2,1)S(1)}, u32[]{:S(2)}, u32[]{:S(2)}) %collective-permute-start.22) | collective-permute-done | bytes 589856 | tf_op jit(solution)/shard_map/ppermute | solution.py:21
  363.2 4.5 %fusion.11 = bf16[589824]{0:T(1024)(128)(2,1)S(1)} fusion(s32[]{:T(128)S(6)} %select_n.100, bf16[589824]{0:T(1024)(128)(2,1)S(1)} %constant_dynamic-update-slice_fusion.31), kind=kLoop, calls=%fused_computation.35 | loop fusion | flops 2359296 | bytes 2359300 | tf_op jit(solution)/shard_map/jit(_roll_dynamic)/concatenate | solution.py:30
  367.6 8.1 %collective-permute-done.17 = bf16[294912]{0:T(1024)(128)(2,1)S(1)} collective-permute-done((bf16[294912]{0:T(1024)(128)(2,1)S(1)}, bf16[294912]{0:T(1024)(128)(2,1)S(1)}, u32[]{:S(2)}, u32[]{:S(2)}) %collective-permute-start.17) | collective-permute-done | bytes 589856 | tf_op jit(solution)/shard_map/ppermute | solution.py:21
  375.8 5.5 %fusion.12 = bf16[589824]{0:T(1024)(128)(2,1)} fusion(s32[]{:T(128)S(6)} %select_n.100, bf16[589824]{0:T(1024)(128)(2,1)S(1)} %constant_dynamic-update-slice_fusion.30), kind=kLoop, calls=%fused_computation.36 | loop fusion | flops 2359296 | bytes 2359300 | tf_op jit(solution)/shard_map/jit(_roll_dynamic)/concatenate | solution.py:30
  381.7 2.2 stack.189
  384.0 5.2 %collective-permute-done.12 = bf16[311296]{0:T(1024)(128)(2,1)} collective-permute-done((bf16[311296]{0:T(1024)(128)(2,1)}, bf16[311296]{0:T(1024)(128)(2,1)}, u32[]{:S(2)}, u32[]{:S(2)}) %collective-permute-start.12) | collective-permute-done | bytes 622624 | tf_op jit(solution)/shard_map/ppermute | solution.py:21
  389.2 1.9 constant_dynamic-update-slice_fusion.38
  394.4 1.9 constant_dynamic-update-slice_fusion.32
  396.4 2.9 dynamic-slice.3
  399.3 3.0 stack.172
  403.9 3.0 pad_maximum_fusion
  (243 shorter events, 57.8 us)
Async XLA Ops:
  7.2 40.6 %copy-start = (bf16[128,256]{1,0:T(8,128)(2,1)S(1)}, bf16[128,256]{1,0:T(8,128)(2,1)}, u32[]{:S(2)}) copy-start(bf16[128,256]{1,0:T(8,128)(2,1)} %param.12) | copy-start | bytes 196612
  11.2 6.2 %copy-start.6 = (bf16[16,32,256]{2,1,0:T(8,128)(2,1)S(1)}, bf16[16,32,256]{2,1,0:T(8,128)(2,1)}, u32[]{:S(2)}) copy-start(bf16[16,32,256]{2,1,0:T(8,128)(2,1)} %param.15) | copy-start | bytes 786436
  11.2 9.5 %copy-start.25 = (bf16[256]{0:T(256)(128)(2,1)S(1)}, bf16[256]{0:T(256)(128)(2,1)}, u32[]{:S(2)}) copy-start(bf16[256]{0:T(256)(128)(2,1)} %param.13) | copy-start | bytes 1540
  11.2 32.4 %all-to-all-start = ((bf16[32,144,128]{2,1,0:T(8,128)(2,1)}), bf16[32,144,128]{2,1,0:T(8,128)(2,1)S(1)}, u32[]{:S(2)}, u32[]{:S(2)}) async-start(bf16[32,144,128]{2,1,0:T(8,128)(2,1)} %pad_maximum_fusion.5), calls=%async_computation | async-start | bytes 2359296 | tf_op jit(solution)/shard_map/all_to_all | solution.py:108
  17.4 284.9 %all-reduce.7.cloned.1.call-start = ((), (), s32[]{:S(2)}) async-start(), calls=%async_computation.2 | async-start | bytes 14417920
  17.5 10.9 %collective-permute-start.5 = (bf16[16,3,256]{2,1,0:T(4,128)(2,1)S(1)}, bf16[16,3,256]{2,1,0:T(4,128)(2,1)S(1)}, u32[]{:S(2)}, u32[]{:S(2)}) collective-permute-start(bf16[16,3,256]{2,1,0:T(4,128)(2,1)S(1)} %get-tuple-element.35), channel_id=1, source_target_pairs={{0,28},{4,0},{8,4},{12,8},{16,12},{20,16},{24,20},{28,24},{1,29},{... | collective-permute-start | bytes 73736 | tf_op jit(solution)/shard_map/ppermute | solution.py:49
  17.9 10.5 %collective-permute-start.4 = (bf16[16,3,256]{2,1,0:T(4,128)(2,1)S(1)}, bf16[16,3,256]{2,1,0:T(4,128)(2,1)S(1)}, u32[]{:S(2)}, u32[]{:S(2)}) collective-permute-start(bf16[16,3,256]{2,1,0:T(4,128)(2,1)S(1)} %get-tuple-element.34), channel_id=1, source_target_pairs={{0,4},{4,8},{8,12},{12,16},{16,20},{20,24},{24,28},{28,0},{1,5},{5... | collective-permute-start | bytes 73736 | tf_op jit(solution)/shard_map/ppermute | solution.py:48
  20.7 40.2 %copy-start.20 = (pred[22]{0:T(512)(128)(4,1)}, pred[22]{0:T(512)(128)(4,1)S(1)}, u32[]{:S(2)}) copy-start(pred[22]{0:T(512)(128)(4,1)S(1)} %compare_and_fusion.4) | copy-start | bytes 70
  47.7 11.8 %copy-start.14 = (bf16[512,128]{1,0:T(8,128)(2,1)}, bf16[512,128]{1,0:T(8,128)(2,1)S(1)}, u32[]{:S(2)}) copy-start(bf16[512,128]{1,0:T(8,128)(2,1)S(1)} %fusion.21) | copy-start | bytes 393220
  48.0 7.4 %collective-permute-start.1 = (bf16[16,6,256]{2,1,0:T(8,128)(2,1)S(1)}, bf16[16,6,256]{2,1,0:T(8,128)(2,1)S(1)}, u32[]{:S(2)}, u32[]{:S(2)}) collective-permute-start(bf16[16,6,256]{2,1,0:T(8,128)(2,1)S(1)} %get-tuple-element.37), channel_id=1, source_target_pairs={{0,28},{4,0},{8,4},{12,8},{16,12},{20,16},{24,20},{28,24},{1,29},{... | collective-permute-start | bytes 147464 | tf_op jit(solution)/shard_map/ppermute | solution.py:49
  49.6 5.9 %collective-permute-start = (bf16[16,6,256]{2,1,0:T(8,128)(2,1)S(1)}, bf16[16,6,256]{2,1,0:T(8,128)(2,1)S(1)}, u32[]{:S(2)}, u32[]{:S(2)}) collective-permute-start(bf16[16,6,256]{2,1,0:T(8,128)(2,1)S(1)} %get-tuple-element.36), channel_id=1, source_target_pairs={{0,4},{4,8},{8,12},{12,16},{16,20},{20,24},{24,28},{28,0},{1,5},{5... | collective-permute-start | bytes 147464 | tf_op jit(solution)/shard_map/ppermute | solution.py:48
  50.7 10.8 %collective-permute-start.7 = (bf16[3,38,256]{2,1,0:T(8,128)(2,1)S(1)}, bf16[3,38,256]{2,1,0:T(8,128)(2,1)S(1)}, u32[]{:S(2)}, u32[]{:S(2)}) collective-permute-start(bf16[3,38,256]{2,1,0:T(8,128)(2,1)S(1)} %get-tuple-element.27), channel_id=1, source_target_pairs={{1,0},{2,1},{3,2},{5,4},{6,5},{7,6},{9,8},{10,9},{11,10},{13,12},{... | collective-permute-start | bytes 175112 | tf_op jit(solution)/shard_map/ppermute | solution.py:52
  54.1 7.4 %collective-permute-start.6 = (bf16[3,38,256]{2,1,0:T(8,128)(2,1)S(1)}, bf16[3,38,256]{2,1,0:T(8,128)(2,1)S(1)}, u32[]{:S(2)}, u32[]{:S(2)}) collective-permute-start(bf16[3,38,256]{2,1,0:T(8,128)(2,1)S(1)} %get-tuple-element.26), channel_id=1, source_target_pairs={{0,1},{1,2},{2,3},{4,5},{5,6},{6,7},{8,9},{9,10},{10,11},{12,13},{... | collective-permute-start | bytes 175112 | tf_op jit(solution)/shard_map/ppermute | solution.py:51
  55.5 11.2 %copy-start.12 = (bf16[16,6,256]{2,1,0:T(8,128)(2,1)}, bf16[16,6,256]{2,1,0:T(8,128)(2,1)S(1)}, u32[]{:S(2)}) copy-start(bf16[16,6,256]{2,1,0:T(8,128)(2,1)S(1)} %collective-permute-done) | copy-start | bytes 147460
  55.6 6.9 %collective-permute-start.3 = (bf16[6,44,256]{2,1,0:T(8,128)(2,1)S(1)}, bf16[6,44,256]{2,1,0:T(8,128)(2,1)S(1)}, u32[]{:S(2)}, u32[]{:S(2)}) collective-permute-start(bf16[6,44,256]{2,1,0:T(8,128)(2,1)S(1)} %get-tuple-element.23), channel_id=1, source_target_pairs={{1,0},{2,1},{3,2},{5,4},{6,5},{7,6},{9,8},{10,9},{11,10},{13,12},{... | collective-permute-start | bytes 405512 | tf_op jit(solution)/shard_map/ppermute | solution.py:52
  59.6 6.9 %collective-permute-start.2 = (bf16[6,44,256]{2,1,0:T(8,128)(2,1)S(1)}, bf16[6,44,256]{2,1,0:T(8,128)(2,1)S(1)}, u32[]{:S(2)}, u32[]{:S(2)}) collective-permute-start(bf16[6,44,256]{2,1,0:T(8,128)(2,1)S(1)} %get-tuple-element.22), channel_id=1, source_target_pairs={{0,1},{1,2},{2,3},{4,5},{5,6},{6,7},{8,9},{9,10},{10,11},{12,13},{... | collective-permute-start | bytes 405512 | tf_op jit(solution)/shard_map/ppermute | solution.py:51
  61.5 5.4 %copy-start.16 = (bf16[3,38,256]{2,1,0:T(8,128)(2,1)}, bf16[3,38,256]{2,1,0:T(8,128)(2,1)S(1)}, u32[]{:S(2)}) copy-start(bf16[3,38,256]{2,1,0:T(8,128)(2,1)S(1)} %collective-permute-done.7) | copy-start | bytes 175108
  61.5 5.4 %copy-start.18 = (bf16[3,38,256]{2,1,0:T(8,128)(2,1)}, bf16[3,38,256]{2,1,0:T(8,128)(2,1)S(1)}, u32[]{:S(2)}) copy-start(bf16[3,38,256]{2,1,0:T(8,128)(2,1)S(1)} %collective-permute-done.6) | copy-start | bytes 175108
  71.4 1.1 copy-start.22
  74.0 1.7 copy-start.30
  79.3 2.0 copy-start.24
  80.0 1.3 copy-start.29
  83.4 1.0 copy-start.1
  83.4 1.0 copy-start.23
  88.8 1.0 copy-start.7
  88.8 1.0 copy-start.17
  117.7 39.6 %all-to-all-start.1 = ((bf16[32,128,128]{2,1,0:T(8,128)(2,1)}), bf16[32,128,128]{2,1,0:T(8,128)(2,1)S(1)}, u32[]{:S(2)}, u32[]{:S(2)}) async-start(bf16[32,128,128]{2,1,0:T(8,128)(2,1)} %bitcast.105), calls=%async_computation.1 | async-start | bytes 2097152 | tf_op jit(solution)/shard_map/all_to_all | solution.py:192
  303.2 7.0 %collective-permute-start.18 = (bf16[18432]{0:T(1024)(128)(2,1)S(1)}, bf16[18432]{0:T(1024)(128)(2,1)S(1)}, u32[]{:S(2)}, u32[]{:S(2)}) collective-permute-start(bf16[18432]{0:T(1024)(128)(2,1)S(1)} %get-tuple-element.13), channel_id=1, source_target_pairs={{0,31},{1,0},{2,1},{3,2},{4,3},{5,4},{6,5},{7,6},{8,7},{9,8},{10,9... | collective-permute-start | bytes 110600 | tf_op jit(solution)/shard_map/ppermute | solution.py:21
  305.1 7.0 %collective-permute-start.13 = (bf16[18432]{0:T(1024)(128)(2,1)S(1)}, bf16[18432]{0:T(1024)(128)(2,1)S(1)}, u32[]{:S(2)}, u32[]{:S(2)}) collective-permute-start(bf16[18432]{0:T(1024)(128)(2,1)S(1)} %get-tuple-element.11), channel_id=1, source_target_pairs={{0,31},{1,0},{2,1},{3,2},{4,3},{5,4},{6,5},{7,6},{8,7},{9,8},{10,9... | collective-permute-start | bytes 110600 | tf_op jit(solution)/shard_map/ppermute | solution.py:21
  306.9 7.1 %collective-permute-start.8 = (bf16[19456]{0:T(1024)(128)(2,1)S(1)}, bf16[19456]{0:T(1024)(128)(2,1)S(1)}, u32[]{:S(2)}, u32[]{:S(2)}) collective-permute-start(bf16[19456]{0:T(1024)(128)(2,1)S(1)} %get-tuple-element.9), channel_id=1, source_target_pairs={{0,31},{1,0},{2,1},{3,2},{4,3},{5,4},{6,5},{7,6},{8,7},{9,8},{10,9... | collective-permute-start | bytes 116744 | tf_op jit(solution)/shard_map/ppermute | solution.py:21
  310.2 11.9 %collective-permute-start.19 = (bf16[36864]{0:T(1024)(128)(2,1)S(1)}, bf16[36864]{0:T(1024)(128)(2,1)S(1)}, u32[]{:S(2)}, u32[]{:S(2)}) collective-permute-start(bf16[36864]{0:T(1024)(128)(2,1)S(1)} %pad_maximum_fusion.25), channel_id=1, source_target_pairs={{0,30},{1,31},{2,0},{3,1},{4,2},{5,3},{6,4},{7,5},{8,6},{9,7},{10,... | collective-permute-start | bytes 221192 | tf_op jit(solution)/shard_map/ppermute | solution.py:21
  312.1 11.6 %collective-permute-start.14 = (bf16[36864]{0:T(1024)(128)(2,1)S(1)}, bf16[36864]{0:T(1024)(128)(2,1)S(1)}, u32[]{:S(2)}, u32[]{:S(2)}) collective-permute-start(bf16[36864]{0:T(1024)(128)(2,1)S(1)} %pad_maximum_fusion.24), channel_id=1, source_target_pairs={{0,30},{1,31},{2,0},{3,1},{4,2},{5,3},{6,4},{7,5},{8,6},{9,7},{10,... | collective-permute-start | bytes 221192 | tf_op jit(solution)/shard_map/ppermute | solution.py:21
  314.1 10.6 %collective-permute-start.9 = (bf16[38912]{0:T(1024)(128)(2,1)S(1)}, bf16[38912]{0:T(1024)(128)(2,1)S(1)}, u32[]{:S(2)}, u32[]{:S(2)}) collective-permute-start(bf16[38912]{0:T(1024)(128)(2,1)S(1)} %pad_maximum_fusion.23), channel_id=1, source_target_pairs={{0,30},{1,31},{2,0},{3,1},{4,2},{5,3},{6,4},{7,5},{8,6},{9,7},{10,... | collective-permute-start | bytes 233480 | tf_op jit(solution)/shard_map/ppermute | solution.py:21
  322.1 5.5 %collective-permute-start.20 = (bf16[73728]{0:T(1024)(128)(2,1)S(1)}, bf16[73728]{0:T(1024)(128)(2,1)S(1)}, u32[]{:S(2)}, u32[]{:S(2)}) collective-permute-start(bf16[73728]{0:T(1024)(128)(2,1)S(1)} %pad_maximum_fusion.22), channel_id=1, source_target_pairs={{0,28},{1,29},{2,30},{3,31},{4,0},{5,1},{6,2},{7,3},{8,4},{9,5},{1... | collective-permute-start | bytes 442376 | tf_op jit(solution)/shard_map/ppermute | solution.py:21
  323.7 5.5 %collective-permute-start.15 = (bf16[73728]{0:T(1024)(128)(2,1)S(1)}, bf16[73728]{0:T(1024)(128)(2,1)S(1)}, u32[]{:S(2)}, u32[]{:S(2)}) collective-permute-start(bf16[73728]{0:T(1024)(128)(2,1)S(1)} %pad_maximum_fusion.21), channel_id=1, source_target_pairs={{0,28},{1,29},{2,30},{3,31},{4,0},{5,1},{6,2},{7,3},{8,4},{9,5},{1... | collective-permute-start | bytes 442376 | tf_op jit(solution)/shard_map/ppermute | solution.py:21
  324.7 6.2 %copy-start.10 = (bf16[38912]{0:T(1024)(128)(2,1)}, bf16[38912]{0:T(1024)(128)(2,1)S(1)}, u32[]{:S(2)}) copy-start(bf16[38912]{0:T(1024)(128)(2,1)S(1)} %collective-permute-done.9) | copy-start | bytes 233476
  324.7 6.2 %collective-permute-start.10 = (bf16[77824]{0:T(1024)(128)(2,1)S(1)}, bf16[77824]{0:T(1024)(128)(2,1)S(1)}, u32[]{:S(2)}, u32[]{:S(2)}) collective-permute-start(bf16[77824]{0:T(1024)(128)(2,1)S(1)} %pad_maximum_fusion.17), channel_id=1, source_target_pairs={{0,28},{1,29},{2,30},{3,31},{4,0},{5,1},{6,2},{7,3},{8,4},{9,5},{1... | collective-permute-start | bytes 466952 | tf_op jit(solution)/shard_map/ppermute | solution.py:21
  327.7 10.0 %collective-permute-start.21 = (bf16[147456]{0:T(1024)(128)(2,1)S(1)}, bf16[147456]{0:T(1024)(128)(2,1)S(1)}, u32[]{:S(2)}, u32[]{:S(2)}) collective-permute-start(bf16[147456]{0:T(1024)(128)(2,1)S(1)} %pad_maximum_fusion.12), channel_id=1, source_target_pairs={{0,24},{1,25},{2,26},{3,27},{4,28},{5,29},{6,30},{7,31},{8,0},{9,1... | collective-permute-start | bytes 884744 | tf_op jit(solution)/shard_map/ppermute | solution.py:21
  329.3 14.8 %collective-permute-start.16 = (bf16[147456]{0:T(1024)(128)(2,1)S(1)}, bf16[147456]{0:T(1024)(128)(2,1)S(1)}, u32[]{:S(2)}, u32[]{:S(2)}) collective-permute-start(bf16[147456]{0:T(1024)(128)(2,1)S(1)} %pad_maximum_fusion.11), channel_id=1, source_target_pairs={{0,24},{1,25},{2,26},{3,27},{4,28},{5,29},{6,30},{7,31},{8,0},{9,1... | collective-permute-start | bytes 884744 | tf_op jit(solution)/shard_map/ppermute | solution.py:21
  330.9 13.2 %copy-start.2 = (bf16[77824]{0:T(1024)(128)(2,1)}, bf16[77824]{0:T(1024)(128)(2,1)S(1)}, u32[]{:S(2)}) copy-start(bf16[77824]{0:T(1024)(128)(2,1)S(1)} %collective-permute-done.10) | copy-start | bytes 466948
  330.9 19.4 %collective-permute-start.11 = (bf16[155648]{0:T(1024)(128)(2,1)S(1)}, bf16[155648]{0:T(1024)(128)(2,1)S(1)}, u32[]{:S(2)}, u32[]{:S(2)}) collective-permute-start(bf16[155648]{0:T(1024)(128)(2,1)S(1)} %pad_maximum_fusion.10), channel_id=1, source_target_pairs={{0,24},{1,25},{2,26},{3,27},{4,28},{5,29},{6,30},{7,31},{8,0},{9,1... | collective-permute-start | bytes 933896 | tf_op jit(solution)/shard_map/ppermute | solution.py:21
  337.8 25.3 %collective-permute-start.22 = (bf16[294912]{0:T(1024)(128)(2,1)S(1)}, bf16[294912]{0:T(1024)(128)(2,1)S(1)}, u32[]{:S(2)}, u32[]{:S(2)}) collective-permute-start(bf16[294912]{0:T(1024)(128)(2,1)S(1)} %get-tuple-element.32), channel_id=1, source_target_pairs={{0,16},{1,17},{2,18},{3,19},{4,20},{5,21},{6,22},{7,23},{8,24},{9,... | collective-permute-start | bytes 1769480 | tf_op jit(solution)/shard_map/ppermute | solution.py:21
  344.1 31.6 %collective-permute-start.17 = (bf16[294912]{0:T(1024)(128)(2,1)S(1)}, bf16[294912]{0:T(1024)(128)(2,1)S(1)}, u32[]{:S(2)}, u32[]{:S(2)}) collective-permute-start(bf16[294912]{0:T(1024)(128)(2,1)S(1)} %get-tuple-element.30), channel_id=1, source_target_pairs={{0,16},{1,17},{2,18},{3,19},{4,20},{5,21},{6,22},{7,23},{8,24},{9,... | collective-permute-start | bytes 1769480 | tf_op jit(solution)/shard_map/ppermute | solution.py:21
  350.3 17.3 %copy-start.8 = (bf16[155648]{0:T(1024)(128)(2,1)}, bf16[155648]{0:T(1024)(128)(2,1)S(1)}, u32[]{:S(2)}) copy-start(bf16[155648]{0:T(1024)(128)(2,1)S(1)} %collective-permute-done.11) | copy-start | bytes 933892
  351.3 37.9 %collective-permute-start.12 = (bf16[311296]{0:T(1024)(128)(2,1)}, bf16[311296]{0:T(1024)(128)(2,1)}, u32[]{:S(2)}, u32[]{:S(2)}) collective-permute-start(bf16[311296]{0:T(1024)(128)(2,1)} %get-tuple-element.28), channel_id=1, source_target_pairs={{0,16},{1,17},{2,18},{3,19},{4,20},{5,21},{6,22},{7,23},{8,24},{9,... | collective-permute-start | bytes 1867784 | tf_op jit(solution)/shard_map/ppermute | solution.py:21
  383.9 8.5 %copy-start.11 = (bf16[38912]{0:T(1024)(128)(2,1)S(1)}, bf16[38912]{0:T(1024)(128)(2,1)}, u32[]{:S(2)}) copy-start(bf16[38912]{0:T(1024)(128)(2,1)} %copy-done.10) | copy-start | bytes 233476
  383.9 9.1 %copy-start.3 = (bf16[77824]{0:T(1024)(128)(2,1)S(1)}, bf16[77824]{0:T(1024)(128)(2,1)}, u32[]{:S(2)}) copy-start(bf16[77824]{0:T(1024)(128)(2,1)} %copy-done.2) | copy-start | bytes 466948
  383.9 9.8 %copy-start.9 = (bf16[155648]{0:T(1024)(128)(2,1)S(1)}, bf16[155648]{0:T(1024)(128)(2,1)}, u32[]{:S(2)}) copy-start(bf16[155648]{0:T(1024)(128)(2,1)} %copy-done.8) | copy-start | bytes 933892
  (10 other events, 8.0 us)
Sparse Core Ops, SparseCore 0:
  115.1 187.1 all-reduce.6
